TPU v7x, 256 devices: a whole 4x4x8 slice. The times are simulated.
256 devices in a mesh: seq: 32 (over x_hi, z, core), tensor: 8 (over y, x_lo).
Axes of the slice: x: 4 (x_hi: 2, x_lo: 2; x = x_hi * 2 + x_lo), y: 4, z: 8, core: 2. Of those that a mesh axis runs over, the one named last changes fastest.
Arguments:
- tokens: bfloat16 [4, 1024, 4096], P(None, 'seq', 'tensor'), may hold values from -600 to 600
- norm_gain: bfloat16 [4096], replicated, may hold values from 0.099609375 to 1.8984375
- w_query: bfloat16 [4096, 2048], P(None, 'tensor'), may hold values from -0.1875 to 0.1875
- w_key: bfloat16 [4096, 2048], P(None, 'tensor'), may hold values from -0.09375 to 0.09375
- w_value: bfloat16 [4096, 2048], P(None, 'tensor'), may hold values from -0.09375 to 0.09375
- w_out: bfloat16 [2048, 4096], P('tensor'), may hold values from -1 to 1
- cache_keys: bfloat16 [4, 8192, 2048], P(None, 'seq', 'tensor'), may hold values from -103 to 103
- cache_values: bfloat16 [4, 8192, 2048], P(None, 'seq', 'tensor'), may hold values from -6 to 6
- cache_len: int32 [4], replicated, may hold values from 1 to 8192, as said below
- group_len: int32 [4], replicated, may hold values from 1 to 1024, 3584 in all
Outputs:
- mixed: bfloat16 [4, 1024, 4096], P(None, 'seq', 'tensor')
- new_keys: bfloat16 [4, 1024, 2048], P(None, 'seq', 'tensor')
- new_values: bfloat16 [4, 1024, 2048], P(None, 'seq', 'tensor')
Inputs may be any that keep to these rules, and one draw needn't show every extreme that they name: `cache_len`: one request's cache holds all 8192 positions. `group_len`: the new-token counts sum to 3584.
All inputs are finite; a program needn't handle non-finite values.
Results may differ from a plain program's by a relative error of at most 0.0075.
The roundings to bfloat16 on the way count: a program that leaves them out, or rounds other values in their place, can miss the bound.
Values may be sent and summed in bfloat16 or wider, within the bound.
No kernel may reach another device: no remote copies, remote signals or barrier semaphores. Data moves between devices by JAX's collectives and lax.ppermute only.
A program may use at most 128 MiB of HBM per device.

v0:
```python
import jax
import jax.numpy as jnp
from jax import lax
from jax.sharding import PartitionSpec as P

HD = 128


def rotate(vector, position):
    half_dim = vector.shape[-1] // 2
    frequency = 1000000.0 ** (-(jnp.arange(half_dim, dtype=jnp.float32) * 2.0 / vector.shape[-1]))
    angles = position.astype(jnp.float32)[..., None] * frequency
    cosine = jnp.concatenate([jnp.cos(angles), jnp.cos(angles)], -1)[..., None, :]
    sine = jnp.concatenate([jnp.sin(angles), jnp.sin(angles)], -1)[..., None, :]
    turned = jnp.concatenate([-vector[..., half_dim:], vector[..., :half_dim]], -1)
    return vector * cosine + turned * sine


def body(
    tokens,
    norm_gain,
    w_query,
    w_key,
    w_value,
    w_out,
    cache_keys,
    cache_values,
    cache_len,
    group_len,
):
    seq_index = lax.axis_index("seq")
    seq_count = lax.axis_size("seq")
    requests, local_rows, width_part = tokens.shape
    heads_width = w_query.shape[1]
    local_heads = heads_width // HD
    cache_slots = cache_keys.shape[1]
    gain = norm_gain.astype(jnp.float32)
    offsets = jnp.arange(local_rows, dtype=jnp.int32)
    token_index = seq_index * local_rows + offsets
    slot_index = seq_index * cache_slots + jnp.arange(cache_slots, dtype=jnp.int32)
    query_index = jnp.arange(seq_count * local_rows, dtype=jnp.int32)
    score_scale = HD ** (-0.5)
    numer_width = local_rows * heads_width
    mixed_list = []
    key_list = []
    value_list = []
    for request in range(requests):
        gathered = lax.all_gather(tokens[request], "tensor", axis=1, tiled=True).astype(jnp.float32)
        inverse_rms = lax.rsqrt(jnp.mean(gathered * gathered, -1, keepdims=True) + 1e-05)
        normed = (gathered * inverse_rms * gain).astype(jnp.bfloat16)

        def project(weight):
            return jnp.dot(normed, weight, preferred_element_type=jnp.float32).reshape(
                local_rows, local_heads, HD
            )

        position = cache_len[request] + token_index
        queries = rotate(project(w_query)[None], position[None])[0].astype(jnp.bfloat16)
        key_new = rotate(project(w_key)[None], position[None])[0].astype(jnp.bfloat16)
        value_new = project(w_value).astype(jnp.bfloat16)
        live_rows = token_index < group_len[request]
        key_list.append(
            jnp.where(live_rows[:, None], key_new.reshape(local_rows, heads_width), 0.0).astype(
                jnp.bfloat16
            )
        )
        value_list.append(
            jnp.where(live_rows[:, None], value_new.reshape(local_rows, heads_width), 0.0).astype(
                jnp.bfloat16
            )
        )
        all_queries = lax.all_gather(queries, "seq", axis=0, tiled=True)
        cache_k = cache_keys[request].reshape(cache_slots, local_heads, HD)
        cache_v = cache_values[request].reshape(cache_slots, local_heads, HD)
        cache_ok = (slot_index < cache_len[request])[None, None, :]
        group_ok = ((token_index[None, :] <= query_index[:, None]) & live_rows[None, :])[None]
        cache_scores = jnp.where(
            cache_ok,
            jnp.einsum("qhd,khd->hqk", all_queries, cache_k, preferred_element_type=jnp.float32)
            * score_scale,
            -1e30,
        )
        group_scores = jnp.where(
            group_ok,
            jnp.einsum("qhd,khd->hqk", all_queries, key_new, preferred_element_type=jnp.float32)
            * score_scale,
            -1e30,
        )
        row_peak = jnp.maximum(jnp.max(cache_scores, -1), jnp.max(group_scores, -1))
        cache_weights = jnp.where(cache_ok, jnp.exp(cache_scores - row_peak[..., None]), 0.0)
        group_weights = jnp.where(group_ok, jnp.exp(group_scores - row_peak[..., None]), 0.0)
        row_mass = jnp.sum(cache_weights, -1) + jnp.sum(group_weights, -1)
        numerators = jnp.einsum(
            "hqk,khd->qhd",
            cache_weights.astype(jnp.bfloat16),
            cache_v,
            preferred_element_type=jnp.float32,
        ) + jnp.einsum(
            "hqk,khd->qhd",
            group_weights.astype(jnp.bfloat16),
            value_new,
            preferred_element_type=jnp.float32,
        )
        stats = jnp.stack([row_peak.T, row_mass.T], -1)
        payload = jnp.concatenate(
            [
                numerators.reshape(seq_count, numer_width),
                stats.reshape(seq_count, local_rows * local_heads * 2),
            ],
            -1,
        )
        received = lax.all_to_all(payload, "seq", 0, 0, tiled=True)
        block_numer = received[:, :numer_width].reshape(seq_count, local_rows, local_heads, HD)
        block_stats = received[:, numer_width:].reshape(seq_count, local_rows, local_heads, 2)
        block_peak = block_stats[..., 0]
        factor = jnp.exp(block_peak - jnp.max(block_peak, 0))
        numer_sum = jnp.sum(block_numer * factor[..., None], 0)
        mass_sum = jnp.sum(block_stats[..., 1] * factor, 0)
        attended = numer_sum / mass_sum[..., None]
        attended = (
            jnp.where(live_rows[:, None, None], attended, 0.0)
            .astype(jnp.bfloat16)
            .reshape(local_rows, heads_width)
        )
        partial_out = jnp.dot(attended, w_out, preferred_element_type=jnp.float32)
        mixed_list.append(
            lax.psum_scatter(partial_out, "tensor", scatter_dimension=1, tiled=True).astype(
                jnp.bfloat16
            )
        )
    return (jnp.stack(mixed_list), jnp.stack(key_list), jnp.stack(value_list))


def solution(mesh):
    placed = (
        P(None, "seq", "tensor"),
        P(),
        P(None, "tensor"),
        P(None, "tensor"),
        P(None, "tensor"),
        P("tensor", None),
        P(None, "seq", "tensor"),
        P(None, "seq", "tensor"),
        P(),
        P(),
    )
    return jax.shard_map(
        body,
        mesh=mesh,
        in_specs=placed,
        out_specs=(P(None, "seq", "tensor"), P(None, "seq", "tensor"), P(None, "seq", "tensor")),
        check_vma=False,
    )
```

profile of v0, /device:TPU:4, one launch (start us, length us, event | category | flops | bytes accessed | tf_op | source)
XLA Modules:
  0.0 626.7 jit_solution(12570984559530962175)
XLA Ops:
  15.1 29.1 %all-gather = bf16[1,32,4096]{2,1,0:T(8,128)(2,1)S(1)} all-gather(bf16[1,32,512]{2,1,0:T(8,128)(2,1)S(1)} %get-tuple-element.11), channel_id=2, replica_groups=mesh['seq'=32,'tensor'=8] {'tensor'}, dimensions={2}, use_global_device_ids=true | all-gather | bytes 294912 | tf_op jit(solution)/shard_map/all_gather | solution.py:48
  49.6 43.6 %all_gather.25 = bf16[1024,2,128]{2,0,1:T(8,128)(2,1)S(1)} all-gather(bf16[32,2,128]{2,0,1:T(8,128)(2,1)S(1)} %get-tuple-element.44), channel_id=1, replica_groups=mesh['seq'=32,'tensor'=8] {'seq'}, dimensions={0}, use_global_device_ids=true | all-gather | bytes 540672 | tf_op jit(solution)/shard_map/all_gather | solution.py:72
  117.1 2.5 reshape.926
  121.8 7.4 %all-to-all-start = ((f32[32,1,8320]{2,1,0:T(1,128)}), f32[32,1,8320]{2,1,0:T(1,128)}, u32[]{:S(2)}, u32[]{:S(2)}) async-start(f32[32,1,8320]{2,1,0:T(1,128)} %copy.234), calls=%async_computation | async-start | bytes 2129920 | tf_op jit(solution)/shard_map/all_to_all | solution.py:112
  129.2 30.6 %all-gather.1 = bf16[1,32,4096]{2,1,0:T(8,128)(2,1)S(1)} all-gather(bf16[1,32,512]{2,1,0:T(8,128)(2,1)S(1)} %copy-done.49), channel_id=3, replica_groups=mesh['seq'=32,'tensor'=8] {'tensor'}, dimensions={2}, use_global_device_ids=true | all-gather | bytes 294912 | tf_op jit(solution)/shard_map/all_gather | solution.py:48
  159.9 2.2 fusion.211
  165.1 29.0 %all-gather.2 = bf16[1,32,4096]{2,1,0:T(8,128)(2,1)S(1)} all-gather(bf16[1,32,512]{2,1,0:T(8,128)(2,1)S(1)} %copy-done.48), channel_id=4, replica_groups=mesh['seq'=32,'tensor'=8] {'tensor'}, dimensions={2}, use_global_device_ids=true | all-gather | bytes 294912 | tf_op jit(solution)/shard_map/all_gather | solution.py:48
  198.8 28.7 %all-gather.3 = bf16[1,32,4096]{2,1,0:T(8,128)(2,1)S(1)} all-gather(bf16[1,32,512]{2,1,0:T(8,128)(2,1)S(1)} %copy-done.47), channel_id=5, replica_groups=mesh['seq'=32,'tensor'=8] {'tensor'}, dimensions={2}, use_global_device_ids=true | all-gather | bytes 294912 | tf_op jit(solution)/shard_map/all_gather | solution.py:48
  230.6 39.5 %all_gather.27 = bf16[1024,2,128]{2,0,1:T(8,128)(2,1)S(1)} all-gather(bf16[32,2,128]{2,0,1:T(8,128)(2,1)S(1)} %get-tuple-element.46), channel_id=1, replica_groups=mesh['seq'=32,'tensor'=8] {'seq'}, dimensions={0}, use_global_device_ids=true | all-gather | bytes 540672 | tf_op jit(solution)/shard_map/all_gather | solution.py:72
  284.3 3.1 reshape.929
  291.5 38.3 %all_gather.29 = bf16[1024,2,128]{2,0,1:T(8,128)(2,1)S(1)} all-gather(bf16[32,2,128]{2,0,1:T(8,128)(2,1)S(1)} %get-tuple-element.48), channel_id=1, replica_groups=mesh['seq'=32,'tensor'=8] {'seq'}, dimensions={0}, use_global_device_ids=true | all-gather | bytes 540672 | tf_op jit(solution)/shard_map/all_gather | solution.py:72
  347.2 39.4 %all_gather.31 = bf16[1024,2,128]{2,0,1:T(8,128)(2,1)S(1)} all-gather(bf16[32,2,128]{2,0,1:T(8,128)(2,1)S(1)} %get-tuple-element.50), channel_id=1, replica_groups=mesh['seq'=32,'tensor'=8] {'seq'}, dimensions={0}, use_global_device_ids=true | all-gather | bytes 540672 | tf_op jit(solution)/shard_map/all_gather | solution.py:72
  386.7 2.3 maximum_bitcast_fusion.2
  389.0 8.5 %all-to-all-start.1 = ((f32[32,1,8320]{2,1,0:T(1,128)}), f32[32,1,8320]{2,1,0:T(1,128)}, u32[]{:S(2)}, u32[]{:S(2)}) async-start(f32[32,1,8320]{2,1,0:T(1,128)} %copy.253), calls=%async_computation.2 | async-start | bytes 2129920 | tf_op jit(solution)/shard_map/all_to_all | solution.py:112
  397.8 3.4 copy.272
  408.4 2.2 fusion.14
  412.5 12.4 %all-to-all-done.1 = f32[32,1,8320]{2,1,0:T(1,128)} async-done(((f32[32,1,8320]{2,1,0:T(1,128)}), f32[32,1,8320]{2,1,0:T(1,128)}, u32[]{:S(2)}, u32[]{:S(2)}) %all-to-all-start.1) | async-done | bytes 1064992 | tf_op jit(solution)/shard_map/all_to_all | solution.py:112
  424.9 6.7 %all-to-all-start.2 = ((f32[32,1,8320]{2,1,0:T(1,128)}), f32[32,1,8320]{2,1,0:T(1,128)S(1)}, u32[]{:S(2)}, u32[]{:S(2)}) async-start(f32[32,1,8320]{2,1,0:T(1,128)} %copy.272), calls=%async_computation.4 | async-start | bytes 2129920 | tf_op jit(solution)/shard_map/all_to_all | solution.py:112
  435.0 5.1 copy.235
  441.3 3.3 fusion.3
  446.5 5.1 copy.254
  452.4 6.9 %all-to-all-done.2 = f32[32,1,8320]{2,1,0:T(1,128)S(1)} async-done(((f32[32,1,8320]{2,1,0:T(1,128)}), f32[32,1,8320]{2,1,0:T(1,128)S(1)}, u32[]{:S(2)}, u32[]{:S(2)}) %all-to-all-start.2) | async-done | bytes 1064992 | tf_op jit(solution)/shard_map/all_to_all | solution.py:112
  459.3 7.2 %all-to-all-start.3 = ((f32[32,1,8320]{2,1,0:T(1,128)}), f32[32,1,8320]{2,1,0:T(1,128)}, u32[]{:S(2)}, u32[]{:S(2)}) async-start(f32[32,1,8320]{2,1,0:T(1,128)} %copy.291), calls=%async_computation.6 | async-start | bytes 2129920 | tf_op jit(solution)/shard_map/all_to_all | solution.py:112
  467.2 3.3 fusion.2
  472.4 3.7 copy.273
  477.3 3.3 fusion.1
  482.6 11.5 %all-to-all-done.3 = f32[32,1,8320]{2,1,0:T(1,128)} async-done(((f32[32,1,8320]{2,1,0:T(1,128)}), f32[32,1,8320]{2,1,0:T(1,128)}, u32[]{:S(2)}, u32[]{:S(2)}) %all-to-all-start.3) | async-done | bytes 1064992 | tf_op jit(solution)/shard_map/all_to_all | solution.py:112
  494.1 5.1 copy.292
  500.3 3.3 fusion
  507.6 25.9 %reduce-scatter.7.cloned.1.call-done = f32[32,512]{1,0:T(8,128)} async-done(((f32[32,4096]{1,0:T(8,128)}), f32[32,512]{1,0:T(8,128)}) %reduce-scatter.7.cloned.1.call-update) | async-done | bytes 65552 | tf_op jit(solution)/shard_map/reduce_scatter | solution.py:127
  534.3 41.6 %reduce-scatter.9.cloned.1.call-done = f32[32,512]{1,0:T(8,128)} async-done(((f32[32,4096]{1,0:T(8,128)}), f32[32,512]{1,0:T(8,128)}) %reduce-scatter.9.cloned.1.call-update) | async-done | bytes 65552 | tf_op jit(solution)/shard_map/reduce_scatter | solution.py:127
  576.8 41.4 %reduce-scatter.11.cloned.1.call-done = f32[32,512]{1,0:T(8,128)} async-done(((f32[32,4096]{1,0:T(8,128)}), f32[32,512]{1,0:T(8,128)}) %reduce-scatter.11.cloned.1.call-update) | async-done | bytes 65552 | tf_op jit(solution)/shard_map/reduce_scatter | solution.py:127
  (325 shorter events, 115.4 us)
Async XLA Ops:
  7.2 437.8 %copy-start = (bf16[256,4096]{1,0:T(8,128)(2,1)S(1)}, bf16[256,4096]{1,0:T(8,128)(2,1)}, u32[]{:S(2)}) copy-start(bf16[256,4096]{1,0:T(8,128)(2,1)} %param.15) | copy-start | bytes 6291460
  12.9 36.0 %copy-start.21 = (f32[32,128]{1,0:T(8,128)}, f32[32,128]{1,0:T(8,128)S(1)}, u32[]{:S(2)}) copy-start(f32[32,128]{1,0:T(8,128)S(1)} %maximum_bitcast_fusion.4) | copy-start | bytes 49156
  12.9 36.0 %copy-start.37 = (f32[32,128]{1,0:T(8,128)}, f32[32,128]{1,0:T(8,128)S(1)}, u32[]{:S(2)}) copy-start(f32[32,128]{1,0:T(8,128)S(1)} %maximum_bitcast_fusion.5) | copy-start | bytes 49156
  46.4 54.1 %copy-start.11 = (bf16[4,256,256]{2,1,0:T(8,128)(2,1)S(1)}, bf16[4,256,256]{2,1,0:T(8,128)(2,1)}, u32[]{:S(2)}) copy-start(bf16[4,256,256]{2,1,0:T(8,128)(2,1)} %param.16) | copy-start | bytes 1572868
  48.9 55.3 %copy-start.19 = (f32[32,2,64]{2,0,1:T(8,128)}, f32[32,2,64]{2,0,1:T(8,128)S(1)}, u32[]{:S(2)}) copy-start(f32[32,2,64]{2,0,1:T(8,128)S(1)} %get-tuple-element.118) | copy-start | bytes 49156
  119.7 9.5 %copy-start.49 = (bf16[1,32,512]{2,1,0:T(8,128)(2,1)S(1)}, bf16[1,32,512]{2,1,0:T(8,128)(2,1)}, u32[]{:S(2)}) copy-start(bf16[1,32,512]{2,1,0:T(8,128)(2,1)} %get-tuple-element.12) | copy-start | bytes 98308
  121.8 267.2 %all-to-all-start = ((f32[32,1,8320]{2,1,0:T(1,128)}), f32[32,1,8320]{2,1,0:T(1,128)}, u32[]{:S(2)}, u32[]{:S(2)}) async-start(f32[32,1,8320]{2,1,0:T(1,128)} %copy.234), calls=%async_computation | async-start | bytes 2129920 | tf_op jit(solution)/shard_map/all_to_all | solution.py:112
  129.1 33.0 %copy-start.2 = (bf16[4096,256]{1,0:T(8,128)(2,1)S(1)}, bf16[4096,256]{1,0:T(8,128)(2,1)}, u32[]{:S(2)}) copy-start(bf16[4096,256]{1,0:T(8,128)(2,1)} %param.12) | copy-start | bytes 6291460
  159.9 4.1 copy-start.4
  162.2 108.8 %copy-start.9 = (f32[32,256]{1,0:T(8,128)}, f32[32,256]{1,0:T(8,128)S(1)}, u32[]{:S(2)}) copy-start(f32[32,256]{1,0:T(8,128)S(1)} %fusion.211) | copy-start | bytes 98308
  162.2 32.1 %copy-start.1 = (bf16[4096,256]{1,0:T(8,128)(2,1)S(1)}, bf16[4096,256]{1,0:T(8,128)(2,1)}, u32[]{:S(2)}) copy-start(bf16[4096,256]{1,0:T(8,128)(2,1)} %param.13) | copy-start | bytes 6291460
  228.3 41.8 %copy-start.15 = (bf16[1,256,256]{2,1,0:T(8,128)(2,1)S(1)}, bf16[1,256,256]{2,1,0:T(8,128)(2,1)}, u32[]{:S(2)}) copy-start(bf16[1,256,256]{2,1,0:T(8,128)(2,1)} %get-tuple-element.9) | copy-start | bytes 393220
  228.3 41.9 %copy-start.16 = (bf16[1,256,256]{2,1,0:T(8,128)(2,1)S(1)}, bf16[1,256,256]{2,1,0:T(8,128)(2,1)}, u32[]{:S(2)}) copy-start(bf16[1,256,256]{2,1,0:T(8,128)(2,1)} %get-tuple-element.5) | copy-start | bytes 393220
  229.5 40.6 %copy-start.23 = (f32[32,128]{1,0:T(8,128)}, f32[32,128]{1,0:T(8,128)S(1)}, u32[]{:S(2)}) copy-start(f32[32,128]{1,0:T(8,128)S(1)} %maximum_bitcast_fusion.6) | copy-start | bytes 49156
  229.6 40.5 %copy-start.38 = (f32[32,128]{1,0:T(8,128)}, f32[32,128]{1,0:T(8,128)S(1)}, u32[]{:S(2)}) copy-start(f32[32,128]{1,0:T(8,128)S(1)} %maximum_bitcast_fusion.7) | copy-start | bytes 49156
  229.8 40.2 %copy-start.20 = (f32[32,2,64]{2,0,1:T(8,128)}, f32[32,2,64]{2,0,1:T(8,128)S(1)}, u32[]{:S(2)}) copy-start(f32[32,2,64]{2,0,1:T(8,128)S(1)} %get-tuple-element.114) | copy-start | bytes 49156
  288.2 41.6 %copy-start.13 = (bf16[1,256,256]{2,1,0:T(8,128)(2,1)S(1)}, bf16[1,256,256]{2,1,0:T(8,128)(2,1)}, u32[]{:S(2)}) copy-start(bf16[1,256,256]{2,1,0:T(8,128)(2,1)} %get-tuple-element.8) | copy-start | bytes 393220
  288.2 41.7 %copy-start.14 = (bf16[1,256,256]{2,1,0:T(8,128)(2,1)S(1)}, bf16[1,256,256]{2,1,0:T(8,128)(2,1)}, u32[]{:S(2)}) copy-start(bf16[1,256,256]{2,1,0:T(8,128)(2,1)} %get-tuple-element.4) | copy-start | bytes 393220
  290.4 39.4 %copy-start.25 = (f32[32,128]{1,0:T(8,128)}, f32[32,128]{1,0:T(8,128)S(1)}, u32[]{:S(2)}) copy-start(f32[32,128]{1,0:T(8,128)S(1)} %maximum_bitcast_fusion.8) | copy-start | bytes 49156
  290.5 39.3 %copy-start.39 = (f32[32,128]{1,0:T(8,128)}, f32[32,128]{1,0:T(8,128)S(1)}, u32[]{:S(2)}) copy-start(f32[32,128]{1,0:T(8,128)S(1)} %maximum_bitcast_fusion.9) | copy-start | bytes 49156
  337.5 8.0 %copy-start.17 = (f32[32,256]{1,0:T(8,128)S(1)}, f32[32,256]{1,0:T(8,128)}, u32[]{:S(2)}) copy-start(f32[32,256]{1,0:T(8,128)} %fusion.203) | copy-start | bytes 98308
  345.4 52.1 %copy-start.27 = (f32[32,128]{1,0:T(8,128)}, f32[32,128]{1,0:T(8,128)S(1)}, u32[]{:S(2)}) copy-start(f32[32,128]{1,0:T(8,128)S(1)} %maximum_bitcast_fusion.10) | copy-start | bytes 49156
  389.0 12.2 %copy-start.12 = (bf16[1,256,256]{2,1,0:T(8,128)(2,1)S(1)}, bf16[1,256,256]{2,1,0:T(8,128)(2,1)}, u32[]{:S(2)}) copy-start(bf16[1,256,256]{2,1,0:T(8,128)(2,1)} %get-tuple-element.10) | copy-start | bytes 393220
  389.0 35.9 %all-to-all-start.1 = ((f32[32,1,8320]{2,1,0:T(1,128)}), f32[32,1,8320]{2,1,0:T(1,128)}, u32[]{:S(2)}, u32[]{:S(2)}) async-start(f32[32,1,8320]{2,1,0:T(1,128)} %copy.253), calls=%async_computation.2 | async-start | bytes 2129920 | tf_op jit(solution)/shard_map/all_to_all | solution.py:112
  424.9 34.4 %all-to-all-start.2 = ((f32[32,1,8320]{2,1,0:T(1,128)}), f32[32,1,8320]{2,1,0:T(1,128)S(1)}, u32[]{:S(2)}, u32[]{:S(2)}) async-start(f32[32,1,8320]{2,1,0:T(1,128)} %copy.272), calls=%async_computation.4 | async-start | bytes 2129920 | tf_op jit(solution)/shard_map/all_to_all | solution.py:112
  431.6 75.1 %reduce-scatter.5.cloned.1.call-start = ((), (), s32[]{:S(2)}) async-start(), calls=%async_computation.8 | async-start | bytes 589824 | tf_op jit(solution)/shard_map/reduce_scatter | solution.py:127
  459.3 34.8 %all-to-all-start.3 = ((f32[32,1,8320]{2,1,0:T(1,128)}), f32[32,1,8320]{2,1,0:T(1,128)}, u32[]{:S(2)}, u32[]{:S(2)}) async-start(f32[32,1,8320]{2,1,0:T(1,128)} %copy.291), calls=%async_computation.6 | async-start | bytes 2129920 | tf_op jit(solution)/shard_map/all_to_all | solution.py:112
  466.5 67.0 %reduce-scatter.7.cloned.1.call-start = ((), (), s32[]{:S(2)}) async-start(), calls=%async_computation.9 | async-start | bytes 589824 | tf_op jit(solution)/shard_map/reduce_scatter | solution.py:127
  467.2 3.7 copy-start.56
  472.2 103.7 %reduce-scatter.9.cloned.1.call-start = ((), (), s32[]{:S(2)}) async-start(), calls=%async_computation.10 | async-start | bytes 589824 | tf_op jit(solution)/shard_map/reduce_scatter | solution.py:127
  477.3 3.7 copy-start.55
  482.4 135.8 %reduce-scatter.11.cloned.1.call-start = ((), (), s32[]{:S(2)}) async-start(), calls=%async_computation.11 | async-start | bytes 589824 | tf_op jit(solution)/shard_map/reduce_scatter | solution.py:127
  (43 other events, 95.7 us)
Sparse Core Ops, SparseCore 0:
  446.5 43.2 reduce-scatter.4
  492.3 41.1 reduce-scatter.6
  536.0 39.8 reduce-scatter.8
  578.3 39.8 reduce-scatter.10
where the time goes:
time: 637 us; the launch traced here: 627 us
  blocking collectives  278 us (44%)
  waiting for transfers between devices  140 us (22%)
  local copies, waits for them, and re-layouts  72.8 us (11%)
  other arithmetic  58.1 us (9%)
  matrix products  32 us (5%)
  starting transfers between devices  30.2 us (5%)
  between operations  15.7 us (2%)
    all_gather x4, blocking collectives, body(): all_queries = lax.all_gather(queries, 'seq', axis=0, tiled=True)  161 us
    all_gather x4, blocking collectives, body(): lax.all_gather(tokens[request], 'tensor', axis=1, tiled=True)  117 us
    reduce_scatter x4, waiting for transfers between devices, body(): lax.psum_scatter(partial_out, 'tensor', scatter_dimension=1, tiled=True)  109 us
    all_to_all x4, waiting for transfers between devices, body(): received = lax.all_to_all(payload, 'seq', 0, 0, tiled=True)  30.8 us
    all_to_all x4, starting transfers between devices, body(): received = lax.all_to_all(payload, 'seq', 0, 0, tiled=True)  29.7 us
    all_to_all x8, local copies, waits for them, and re-layouts, body(): received = lax.all_to_all(payload, 'seq', 0, 0, tiled=True)  28.6 us
    dot_general x12, matrix products, project(): jnp.dot(normed, weight, preferred_element_type=jnp.float32)  14.1 us
    reduce_sum x4, other arithmetic, body(): numer_sum = jnp.sum(block_numer * factor[..., None], 0)  13.4 us
  transfers between devices with their start and end apart: 8, of which 6 were waited for; matrix products, arithmetic and copies ran while one was open for 19% of the time, Pallas kernels for 0%

commit v1 on v0

--- a/solution.py
+++ b/solution.py
@@ -69,7 +69,9 @@
                 jnp.bfloat16
             )
         )
-        all_queries = lax.all_gather(queries, "seq", axis=0, tiled=True)
+        all_queries = jnp.concatenate(
+            lax.all_to_all(jnp.stack([queries] * lax.axis_size("seq")), "seq", 0, 0), axis=0
+        )
         cache_k = cache_keys[request].reshape(cache_slots, local_heads, HD)
         cache_v = cache_values[request].reshape(cache_slots, local_heads, HD)
         cache_ok = (slot_index < cache_len[request])[None, None, :]

time: 637 us -> 578 us (0.907)
  blocking collectives: 278 us -> 116 us
  starting transfers between devices: 30.2 us -> 68.9 us
  waiting for transfers between devices: 140 us -> 174 us
  local copies, waits for them, and re-layouts: 72.8 us -> 92 us
  other arithmetic: 58.1 us -> 66.5 us
    all_gather x4 -> x0, blocking collectives: 161 us -> none  [body(): all_queries = lax.all_gather(queries, 'seq', axis=0, tiled=True)]
    all_to_all x0 -> x4, starting transfers between devices: none -> 36.9 us  [body(): lax.all_to_all(jnp.stack([queries] * lax.axis_size('seq')), 'seq', 0, 0)]
    all_to_all x0 -> x4, waiting for transfers between devices: none -> 21.9 us  [body(): lax.all_to_all(jnp.stack([queries] * lax.axis_size('seq')), 'seq', 0, 0)]
    all_to_all x4, waiting for transfers between devices: 30.8 us -> 38.2 us  [body(): received = lax.all_to_all(payload, 'seq', 0, 0, tiled=True)]
  transfers between devices with their start and end apart: 8 -> 12, of which waited for: 6 -> 9; matrix products, arithmetic and copies ran while one was open for 19% -> 30% of each run, Pallas kernels for 0% -> 0%
where the time goes in v1:
time: 578 us; the launch traced here: 568 us
  waiting for transfers between devices  174 us (30%)
  blocking collectives  116 us (20%)
  local copies, waits for them, and re-layouts  92 us (16%)
  starting transfers between devices  68.9 us (12%)
  other arithmetic  66.5 us (12%)
  matrix products  33.8 us (6%)
  between operations  16 us (3%)
    all_gather x4, blocking collectives, body(): lax.all_gather(tokens[request], 'tensor', axis=1, tiled=True)  116 us
    reduce_scatter x4, waiting for transfers between devices, body(): lax.psum_scatter(partial_out, 'tensor', scatter_dimension=1, tiled=True)  114 us
    all_to_all x4, waiting for transfers between devices, body(): received = lax.all_to_all(payload, 'seq', 0, 0, tiled=True)  38.2 us
    all_to_all x4, starting transfers between devices, body(): lax.all_to_all(jnp.stack([queries] * lax.axis_size('seq')), 'seq', 0, 0)  36.9 us
    all_to_all x4, starting transfers between devices, body(): received = lax.all_to_all(payload, 'seq', 0, 0, tiled=True)  31.6 us
    all_to_all x8, local copies, waits for them, and re-layouts, body(): received = lax.all_to_all(payload, 'seq', 0, 0, tiled=True)  26.1 us
    all_to_all x4, waiting for transfers between devices, body(): lax.all_to_all(jnp.stack([queries] * lax.axis_size('seq')), 'seq', 0, 0)  21.9 us
    dot_general x12, matrix products, project(): jnp.dot(normed, weight, preferred_element_type=jnp.float32)  18.4 us
  transfers between devices with their start and end apart: 12, of which 9 were waited for; matrix products, arithmetic and copies ran while one was open for 30% of the time, Pallas kernels for 0%

profile of v1, /device:TPU:4, one launch (start us, length us, event | category | flops | bytes accessed | tf_op | source)
XLA Modules:
  0.0 567.7 jit_solution(16131164307123163412)
XLA Ops:
  13.8 29.1 %all-gather = bf16[1,32,4096]{2,1,0:T(8,128)(2,1)S(1)} all-gather(bf16[1,32,512]{2,1,0:T(8,128)(2,1)S(1)} %get-tuple-element.11), channel_id=2, replica_groups=mesh['seq'=32,'tensor'=8] {'tensor'}, dimensions={2}, use_global_device_ids=true | all-gather | bytes 294912 | tf_op jit(solution)/shard_map/all_gather | solution.py:48
  49.2 11.6 %all-to-all-start = ((bf16[32,32,2,128]{3,1,2,0:T(8,128)(2,1)}), bf16[32,32,2,128]{3,1,2,0:T(8,128)(2,1)}, u32[]{:S(2)}, u32[]{:S(2)}) async-start(bf16[32,32,2,128]{3,1,2,0:T(8,128)(2,1)} %stack.62), calls=%async_computation | async-start | bytes 1048576 | tf_op jit(solution)/shard_map/all_to_all | solution.py:73
  61.5 29.2 %all-gather.1 = bf16[1,32,4096]{2,1,0:T(8,128)(2,1)S(1)} all-gather(bf16[1,32,512]{2,1,0:T(8,128)(2,1)S(1)} %get-tuple-element.12), channel_id=3, replica_groups=mesh['seq'=32,'tensor'=8] {'tensor'}, dimensions={2}, use_global_device_ids=true | all-gather | bytes 294912 | tf_op jit(solution)/shard_map/all_gather | solution.py:48
  96.6 29.0 %all-gather.2 = bf16[1,32,4096]{2,1,0:T(8,128)(2,1)S(1)} all-gather(bf16[1,32,512]{2,1,0:T(8,128)(2,1)S(1)} %get-tuple-element.14), channel_id=4, replica_groups=mesh['seq'=32,'tensor'=8] {'tensor'}, dimensions={2}, use_global_device_ids=true | all-gather | bytes 294912 | tf_op jit(solution)/shard_map/all_gather | solution.py:48
  129.2 28.9 %all-gather.3 = bf16[1,32,4096]{2,1,0:T(8,128)(2,1)S(1)} all-gather(bf16[1,32,512]{2,1,0:T(8,128)(2,1)S(1)} %get-tuple-element.13), channel_id=5, replica_groups=mesh['seq'=32,'tensor'=8] {'tensor'}, dimensions={2}, use_global_device_ids=true | all-gather | bytes 294912 | tf_op jit(solution)/shard_map/all_gather | solution.py:48
  209.7 10.2 %all-to-all-start.2 = ((bf16[32,32,2,128]{3,1,2,0:T(8,128)(2,1)}), bf16[32,32,2,128]{3,1,2,0:T(8,128)(2,1)}, u32[]{:S(2)}, u32[]{:S(2)}) async-start(bf16[32,32,2,128]{3,1,2,0:T(8,128)(2,1)} %stack.67), calls=%async_computation.3 | async-start | bytes 1048576 | tf_op jit(solution)/shard_map/all_to_all | solution.py:73
  234.0 2.9 all-to-all-done.2
  237.9 7.3 %all-to-all-start.4 = ((bf16[32,32,2,128]{3,1,2,0:T(8,128)(2,1)}), bf16[32,32,2,128]{3,1,2,0:T(8,128)(2,1)}, u32[]{:S(2)}, u32[]{:S(2)}) async-start(bf16[32,32,2,128]{3,1,2,0:T(8,128)(2,1)} %stack.72), calls=%async_computation.6 | async-start | bytes 1048576 | tf_op jit(solution)/shard_map/all_to_all | solution.py:73
  251.7 10.6 %all-to-all-done.4 = bf16[32,32,2,128]{3,1,2,0:T(8,128)(2,1)} async-done(((bf16[32,32,2,128]{3,1,2,0:T(8,128)(2,1)}), bf16[32,32,2,128]{3,1,2,0:T(8,128)(2,1)}, u32[]{:S(2)}, u32[]{:S(2)}) %all-to-all-start.4) | async-done | bytes 524320 | tf_op jit(solution)/shard_map/all_to_all | solution.py:73
  263.9 7.7 %all-to-all-start.6 = ((bf16[32,32,2,128]{3,1,2,0:T(8,128)(2,1)}), bf16[32,32,2,128]{3,1,2,0:T(8,128)(2,1)}, u32[]{:S(2)}, u32[]{:S(2)}) async-start(bf16[32,32,2,128]{3,1,2,0:T(8,128)(2,1)} %stack.77), calls=%async_computation.9 | async-start | bytes 1048576 | tf_op jit(solution)/shard_map/all_to_all | solution.py:73
  280.4 8.3 %all-to-all-done.6 = bf16[32,32,2,128]{3,1,2,0:T(8,128)(2,1)} async-done(((bf16[32,32,2,128]{3,1,2,0:T(8,128)(2,1)}), bf16[32,32,2,128]{3,1,2,0:T(8,128)(2,1)}, u32[]{:S(2)}, u32[]{:S(2)}) %all-to-all-start.6) | async-done | bytes 524320 | tf_op jit(solution)/shard_map/all_to_all | solution.py:73
  288.7 6.8 %all-to-all-start.1 = ((f32[32,1,8320]{2,1,0:T(1,128)}), f32[32,1,8320]{2,1,0:T(1,128)S(1)}, u32[]{:S(2)}, u32[]{:S(2)}) async-start(f32[32,1,8320]{2,1,0:T(1,128)} %copy.249), calls=%async_computation.1 | async-start | bytes 2129920 | tf_op jit(solution)/shard_map/all_to_all | solution.py:114
  304.1 3.1 reshape.990
  314.1 8.9 %all-to-all-done.1 = f32[32,1,8320]{2,1,0:T(1,128)S(1)} async-done(((f32[32,1,8320]{2,1,0:T(1,128)}), f32[32,1,8320]{2,1,0:T(1,128)S(1)}, u32[]{:S(2)}, u32[]{:S(2)}) %all-to-all-start.1) | async-done | bytes 1064992 | tf_op jit(solution)/shard_map/all_to_all | solution.py:114
  323.0 7.7 %all-to-all-start.3 = ((f32[32,1,8320]{2,1,0:T(1,128)}), f32[32,1,8320]{2,1,0:T(1,128)}, u32[]{:S(2)}, u32[]{:S(2)}) async-start(f32[32,1,8320]{2,1,0:T(1,128)} %copy.269), calls=%async_computation.4 | async-start | bytes 2129920 | tf_op jit(solution)/shard_map/all_to_all | solution.py:114
  339.2 18.9 %all-to-all-done.3 = f32[32,1,8320]{2,1,0:T(1,128)} async-done(((f32[32,1,8320]{2,1,0:T(1,128)}), f32[32,1,8320]{2,1,0:T(1,128)}, u32[]{:S(2)}, u32[]{:S(2)}) %all-to-all-start.3) | async-done | bytes 1064992 | tf_op jit(solution)/shard_map/all_to_all | solution.py:114
  358.1 7.4 %all-to-all-start.5 = ((f32[32,1,8320]{2,1,0:T(1,128)}), f32[32,1,8320]{2,1,0:T(1,128)}, u32[]{:S(2)}, u32[]{:S(2)}) async-start(f32[32,1,8320]{2,1,0:T(1,128)} %copy.289), calls=%async_computation.7 | async-start | bytes 2129920 | tf_op jit(solution)/shard_map/all_to_all | solution.py:114
  365.6 3.0 copy.307
  368.6 3.1 reshape.994
  375.5 3.8 copy.250
  380.4 3.3 fusion.3
  387.7 5.1 copy.270
  393.6 9.8 %all-to-all-start.7 = ((f32[32,1,8320]{2,1,0:T(1,128)}), f32[32,1,8320]{2,1,0:T(1,128)S(1)}, u32[]{:S(2)}, u32[]{:S(2)}) async-start(f32[32,1,8320]{2,1,0:T(1,128)} %copy.309), calls=%async_computation.10 | async-start | bytes 2129920 | tf_op jit(solution)/shard_map/all_to_all | solution.py:114
  404.1 3.3 fusion.2
  409.3 5.1 copy.290
  415.6 3.3 fusion.1
  420.8 10.3 %all-to-all-done.7 = f32[32,1,8320]{2,1,0:T(1,128)S(1)} async-done(((f32[32,1,8320]{2,1,0:T(1,128)}), f32[32,1,8320]{2,1,0:T(1,128)S(1)}, u32[]{:S(2)}, u32[]{:S(2)}) %all-to-all-start.7) | async-done | bytes 1064992 | tf_op jit(solution)/shard_map/all_to_all | solution.py:114
  431.2 3.8 copy.310
  436.1 3.3 fusion
  443.4 31.1 %reduce-scatter.7.cloned.1.call-done = f32[32,512]{1,0:T(8,128)} async-done(((f32[32,4096]{1,0:T(8,128)}), f32[32,512]{1,0:T(8,128)}) %reduce-scatter.7.cloned.1.call-update) | async-done | bytes 65552 | tf_op jit(solution)/shard_map/reduce_scatter | solution.py:129
  475.4 41.6 %reduce-scatter.9.cloned.1.call-done = f32[32,512]{1,0:T(8,128)} async-done(((f32[32,4096]{1,0:T(8,128)}), f32[32,512]{1,0:T(8,128)}) %reduce-scatter.9.cloned.1.call-update) | async-done | bytes 65552 | tf_op jit(solution)/shard_map/reduce_scatter | solution.py:129
  517.8 41.4 %reduce-scatter.11.cloned.1.call-done = f32[32,512]{1,0:T(8,128)} async-done(((f32[32,4096]{1,0:T(8,128)}), f32[32,512]{1,0:T(8,128)}) %reduce-scatter.11.cloned.1.call-update) | async-done | bytes 65552 | tf_op jit(solution)/shard_map/reduce_scatter | solution.py:129
  (399 shorter events, 152.6 us)
Async XLA Ops:
  7.2 376.9 %copy-start = (bf16[256,4096]{1,0:T(8,128)(2,1)S(1)}, bf16[256,4096]{1,0:T(8,128)(2,1)}, u32[]{:S(2)}) copy-start(bf16[256,4096]{1,0:T(8,128)(2,1)} %param.15) | copy-start | bytes 6291460
  12.2 35.4 %copy-start.54 = (f32[32,128]{1,0:T(8,128)}, f32[32,128]{1,0:T(8,128)S(1)}, u32[]{:S(2)}) copy-start(f32[32,128]{1,0:T(8,128)S(1)} %maximum_bitcast_fusion.4) | copy-start | bytes 49156
  12.3 35.3 %copy-start.67 = (f32[32,128]{1,0:T(8,128)}, f32[32,128]{1,0:T(8,128)S(1)}, u32[]{:S(2)}) copy-start(f32[32,128]{1,0:T(8,128)S(1)} %maximum_bitcast_fusion.5) | copy-start | bytes 49156
  45.2 138.7 %copy-start.24 = (f32[32,256]{1,0:T(8,128)}, f32[32,256]{1,0:T(8,128)S(1)}, u32[]{:S(2)}) copy-start(f32[32,256]{1,0:T(8,128)S(1)} %fusion.216) | copy-start | bytes 98308
  47.6 43.3 %copy-start.37 = (f32[32,2,64]{2,0,1:T(8,128)}, f32[32,2,64]{2,0,1:T(8,128)S(1)}, u32[]{:S(2)}) copy-start(f32[32,2,64]{2,0,1:T(8,128)S(1)} %get-tuple-element.118) | copy-start | bytes 49156
  47.6 45.4 %copy-start.35 = (f32[32,2,64]{2,0,1:T(8,128)}, f32[32,2,64]{2,0,1:T(8,128)S(1)}, u32[]{:S(2)}) copy-start(f32[32,2,64]{2,0,1:T(8,128)S(1)} %get-tuple-element.117) | copy-start | bytes 49156
  49.2 159.5 %all-to-all-start = ((bf16[32,32,2,128]{3,1,2,0:T(8,128)(2,1)}), bf16[32,32,2,128]{3,1,2,0:T(8,128)(2,1)}, u32[]{:S(2)}, u32[]{:S(2)}) async-start(bf16[32,32,2,128]{3,1,2,0:T(8,128)(2,1)} %stack.62), calls=%async_computation | async-start | bytes 1048576 | tf_op jit(solution)/shard_map/all_to_all | solution.py:73
  60.9 32.1 %copy-start.2 = (bf16[4096,256]{1,0:T(8,128)(2,1)S(1)}, bf16[4096,256]{1,0:T(8,128)(2,1)}, u32[]{:S(2)}) copy-start(bf16[4096,256]{1,0:T(8,128)(2,1)} %param.12) | copy-start | bytes 6291460
  93.0 76.2 %copy-start.21 = (f32[32,256]{1,0:T(8,128)}, f32[32,256]{1,0:T(8,128)S(1)}, u32[]{:S(2)}) copy-start(f32[32,256]{1,0:T(8,128)S(1)} %fusion.211) | copy-start | bytes 98308
  94.2 33.9 %copy-start.3 = (bf16[4096,256]{1,0:T(8,128)(2,1)S(1)}, bf16[4096,256]{1,0:T(8,128)(2,1)}, u32[]{:S(2)}) copy-start(bf16[4096,256]{1,0:T(8,128)(2,1)} %param.12) | copy-start | bytes 6291460
  125.8 32.4 %copy-start.1 = (bf16[4096,256]{1,0:T(8,128)(2,1)S(1)}, bf16[4096,256]{1,0:T(8,128)(2,1)}, u32[]{:S(2)}) copy-start(bf16[4096,256]{1,0:T(8,128)(2,1)} %param.13) | copy-start | bytes 6291460
  128.1 45.6 %copy-start.18 = (f32[32,256]{1,0:T(8,128)}, f32[32,256]{1,0:T(8,128)S(1)}, u32[]{:S(2)}) copy-start(f32[32,256]{1,0:T(8,128)S(1)} %fusion.206) | copy-start | bytes 98308
  158.8 19.5 %copy-start.16 = (f32[32,256]{1,0:T(8,128)}, f32[32,256]{1,0:T(8,128)S(1)}, u32[]{:S(2)}) copy-start(f32[32,256]{1,0:T(8,128)S(1)} %fusion.201) | copy-start | bytes 98308
  167.8 19.0 %copy-start.28 = (f32[32,256]{1,0:T(8,128)S(1)}, f32[32,256]{1,0:T(8,128)}, u32[]{:S(2)}) copy-start(f32[32,256]{1,0:T(8,128)} %fusion.213) | copy-start | bytes 98308
  167.8 20.4 %copy-start.29 = (f32[32,256]{1,0:T(8,128)S(1)}, f32[32,256]{1,0:T(8,128)}, u32[]{:S(2)}) copy-start(f32[32,256]{1,0:T(8,128)} %fusion.208) | copy-start | bytes 98308
  167.8 21.8 %copy-start.30 = (f32[32,256]{1,0:T(8,128)S(1)}, f32[32,256]{1,0:T(8,128)}, u32[]{:S(2)}) copy-start(f32[32,256]{1,0:T(8,128)} %fusion.203) | copy-start | bytes 98308
  172.2 19.9 %copy-start.49 = (f32[32,128]{1,0:T(8,128)}, f32[32,128]{1,0:T(8,128)S(1)}, u32[]{:S(2)}) copy-start(f32[32,128]{1,0:T(8,128)S(1)} %maximum_bitcast_fusion.8) | copy-start | bytes 49156
  182.2 24.3 %copy-start.39 = (f32[32,2,64]{2,0,1:T(8,128)}, f32[32,2,64]{2,0,1:T(8,128)S(1)}, u32[]{:S(2)}) copy-start(f32[32,2,64]{2,0,1:T(8,128)S(1)} %get-tuple-element.109) | copy-start | bytes 49156
  183.8 22.7 %copy-start.31 = (f32[32,2,64]{2,0,1:T(8,128)}, f32[32,2,64]{2,0,1:T(8,128)S(1)}, u32[]{:S(2)}) copy-start(f32[32,2,64]{2,0,1:T(8,128)S(1)} %get-tuple-element.105) | copy-start | bytes 49156
  183.8 22.7 %copy-start.33 = (f32[32,2,64]{2,0,1:T(8,128)}, f32[32,2,64]{2,0,1:T(8,128)S(1)}, u32[]{:S(2)}) copy-start(f32[32,2,64]{2,0,1:T(8,128)S(1)} %get-tuple-element.106) | copy-start | bytes 49156
  186.8 36.0 %copy-start.15 = (pred[1024,32]{0,1:T(8,128)(4,1)}, pred[1024,32]{0,1:T(8,128)(4,1)S(1)}, u32[]{:S(2)}) copy-start(pred[1024,32]{0,1:T(8,128)(4,1)S(1)} %get-tuple-element.67) | copy-start | bytes 98308
  209.7 27.2 %all-to-all-start.2 = ((bf16[32,32,2,128]{3,1,2,0:T(8,128)(2,1)}), bf16[32,32,2,128]{3,1,2,0:T(8,128)(2,1)}, u32[]{:S(2)}, u32[]{:S(2)}) async-start(bf16[32,32,2,128]{3,1,2,0:T(8,128)(2,1)} %stack.67), calls=%async_computation.3 | async-start | bytes 1048576 | tf_op jit(solution)/shard_map/all_to_all | solution.py:73
  237.9 24.4 %all-to-all-start.4 = ((bf16[32,32,2,128]{3,1,2,0:T(8,128)(2,1)}), bf16[32,32,2,128]{3,1,2,0:T(8,128)(2,1)}, u32[]{:S(2)}, u32[]{:S(2)}) async-start(bf16[32,32,2,128]{3,1,2,0:T(8,128)(2,1)} %stack.72), calls=%async_computation.6 | async-start | bytes 1048576 | tf_op jit(solution)/shard_map/all_to_all | solution.py:73
  263.9 24.7 %all-to-all-start.6 = ((bf16[32,32,2,128]{3,1,2,0:T(8,128)(2,1)}), bf16[32,32,2,128]{3,1,2,0:T(8,128)(2,1)}, u32[]{:S(2)}, u32[]{:S(2)}) async-start(bf16[32,32,2,128]{3,1,2,0:T(8,128)(2,1)} %stack.77), calls=%async_computation.9 | async-start | bytes 1048576 | tf_op jit(solution)/shard_map/all_to_all | solution.py:73
  288.7 34.3 %all-to-all-start.1 = ((f32[32,1,8320]{2,1,0:T(1,128)}), f32[32,1,8320]{2,1,0:T(1,128)S(1)}, u32[]{:S(2)}, u32[]{:S(2)}) async-start(f32[32,1,8320]{2,1,0:T(1,128)} %copy.249), calls=%async_computation.1 | async-start | bytes 2129920 | tf_op jit(solution)/shard_map/all_to_all | solution.py:114
  323.0 35.1 %all-to-all-start.3 = ((f32[32,1,8320]{2,1,0:T(1,128)}), f32[32,1,8320]{2,1,0:T(1,128)}, u32[]{:S(2)}, u32[]{:S(2)}) async-start(f32[32,1,8320]{2,1,0:T(1,128)} %copy.269), calls=%async_computation.4 | async-start | bytes 2129920 | tf_op jit(solution)/shard_map/all_to_all | solution.py:114
  358.1 35.5 %all-to-all-start.5 = ((f32[32,1,8320]{2,1,0:T(1,128)}), f32[32,1,8320]{2,1,0:T(1,128)}, u32[]{:S(2)}, u32[]{:S(2)}) async-start(f32[32,1,8320]{2,1,0:T(1,128)} %copy.289), calls=%async_computation.7 | async-start | bytes 2129920 | tf_op jit(solution)/shard_map/all_to_all | solution.py:114
  365.5 77.0 %reduce-scatter.5.cloned.1.call-start = ((), (), s32[]{:S(2)}) async-start(), calls=%async_computation.12 | async-start | bytes 589824 | tf_op jit(solution)/shard_map/reduce_scatter | solution.py:129
  393.6 37.6 %all-to-all-start.7 = ((f32[32,1,8320]{2,1,0:T(1,128)}), f32[32,1,8320]{2,1,0:T(1,128)S(1)}, u32[]{:S(2)}, u32[]{:S(2)}) async-start(f32[32,1,8320]{2,1,0:T(1,128)} %copy.309), calls=%async_computation.10 | async-start | bytes 2129920 | tf_op jit(solution)/shard_map/all_to_all | solution.py:114
  403.4 71.1 %reduce-scatter.7.cloned.1.call-start = ((), (), s32[]{:S(2)}) async-start(), calls=%async_computation.13 | async-start | bytes 589824 | tf_op jit(solution)/shard_map/reduce_scatter | solution.py:129
  409.2 107.8 %reduce-scatter.9.cloned.1.call-start = ((), (), s32[]{:S(2)}) async-start(), calls=%async_computation.14 | async-start | bytes 589824 | tf_op jit(solution)/shard_map/reduce_scatter | solution.py:129
  420.7 138.6 %reduce-scatter.11.cloned.1.call-start = ((), (), s32[]{:S(2)}) async-start(), calls=%async_computation.15 | async-start | bytes 589824 | tf_op jit(solution)/shard_map/reduce_scatter | solution.py:129
  (78 other events, 367.8 us)
Sparse Core Ops, SparseCore 0:
  385.6 44.2 reduce-scatter.4
  432.3 42.1 reduce-scatter.6
  477.0 39.8 reduce-scatter.8
  519.3 39.8 reduce-scatter.10
